TPU v7x, 32 devices: a whole 2x2x4 slice. The times are simulated.
32 devices in a mesh: row: 4 (over y, core), col: 8 (over z, x).
Axes of the slice: x: 2, y: 2, z: 4, core: 2. Of those that a mesh axis runs over, the one named last changes fastest.
Arguments:
- tokens: bfloat16 [512, 16384], P('col', 'row'), may hold values from -6 to 6
- gate_packed: bfloat16 [2560, 1024, 128], P('row', 'col'), may hold values from -0.0625 to 0.0625
- up_packed: bfloat16 [2560, 1024, 128], P('row', 'col'), may hold values from -0.0625 to 0.0625
- down_packed: bfloat16 [5120, 512, 128], P('col', 'row'), may hold values from -0.0546875 to 0.0546875
- gate_keep: int32 [128, 208], P('row', 'col'), may hold values from 0 to 1, as said below
- down_keep: int32 [208, 128], P('col', 'row'), may hold values from 0 to 1, as said below
Outputs:
- mixed: bfloat16 [512, 16384], P('col', 'row')
Inputs may be any that keep to these rules, and one draw needn't show every extreme that they name: `gate_keep`: in every tile of 32 x 26 blocks, at least 160 and at most 640 blocks are kept; some tile keeps exactly 640. `down_keep`: in every tile of 26 x 32 blocks, at least 160 and at most 640 blocks are kept; some tile keeps exactly 640.
All inputs are finite; a program needn't handle non-finite values.
Results may differ from a plain program's by a relative error of at most 0.02.
Values may be sent and summed in bfloat16 or wider, within the bound.
No kernel may reach another device: no remote copies, remote signals or barrier semaphores. Data moves between devices by JAX's collectives and lax.ppermute only.
A program may use at most 320 MiB of HBM per device.

v0:
```python
import jax
import jax.numpy as jnp
from jax import lax
from jax.sharding import PartitionSpec as P


def dense_tile(packed_tile, keep_tile):
    in_blocks, out_blocks = keep_tile.shape
    block = packed_tile.shape[2]
    flattened = keep_tile.reshape(-1)
    position = jnp.cumsum(flattened) - 1
    slot_index = jnp.where(flattened == 1, position, 0)
    picked = (
        jnp.take(packed_tile, slot_index, axis=0)
        * flattened.astype(packed_tile.dtype)[:, None, None]
    )
    picked = picked.reshape(in_blocks, out_blocks, block, block).transpose(0, 2, 1, 3)
    return picked.reshape(in_blocks * block, out_blocks * block)


def local(tokens, gate_packed, up_packed, down_packed, gate_keep, down_keep):
    gate_dense = dense_tile(gate_packed, gate_keep)
    up_dense = dense_tile(up_packed, gate_keep)
    down_dense = dense_tile(down_packed, down_keep)
    segment = lax.all_gather(tokens, "col", axis=0, tiled=True)
    gate_rows = jnp.dot(segment, gate_dense, preferred_element_type=jnp.float32)
    up_rows = jnp.dot(segment, up_dense, preferred_element_type=jnp.float32)
    gate_sum, up_sum = (
        lax.psum(gate_rows.astype(jnp.bfloat16), "row").astype(jnp.float32),
        lax.psum(up_rows.astype(jnp.bfloat16), "row").astype(jnp.float32),
    )
    every_hidden = (jax.nn.silu(gate_sum) * up_sum).astype(jnp.bfloat16)
    partial_out = jnp.dot(every_hidden, down_dense, preferred_element_type=jnp.float32)
    summed = lax.psum_scatter(
        partial_out.astype(jnp.bfloat16), "col", scatter_dimension=0, tiled=True
    )
    return summed


def solution(mesh):
    in_specs = (
        P("col", "row"),
        P("row", "col", None),
        P("row", "col", None),
        P("col", "row", None),
        P("row", "col"),
        P("col", "row"),
    )
    out_specs = P("col", "row")
    return jax.shard_map(local, mesh=mesh, in_specs=in_specs, out_specs=out_specs, check_vma=False)
```

profile of v0, /device:TPU:0, one launch (start us, length us, event | category | flops | bytes accessed | tf_op | source)
XLA Modules:
  0.0 474.2 jit_solution(3464177804756279992)
XLA Ops:
  6.5 0.0 all-gather.2.cloned.1.call-start
  6.5 0.7 all-gather.2.cloned.1.call-update
  7.3 0.0 all-reduce.5.cloned.1.call-start
  7.3 0.8 reshape.68
  8.1 0.3 reduce-window.16
  8.4 0.1 slice.20
  8.5 0.1 slice_reduce_fusion.1
  8.6 0.1 add_bitcast_fusion.1
  8.7 27.1 %gather_fusion = bf16[832,128,128]{2,1,0:T(8,128)(2,1)} fusion(bf16[640,128,128]{2,1,0:T(8,128)(2,1)} %param.9, s32[1024]{0:T(1024)S(1)} %pad_clamp_fusion.1), kind=kCustom, calls=%fused_computation.clone | custom fusion | bytes 54529280 | tf_op jit(solution)/shard_map/jit(_take)/gather | solution.py:14
  35.8 27.1 %gather_fusion.1 = bf16[832,128,128]{2,1,0:T(8,128)(2,1)} fusion(bf16[640,128,128]{2,1,0:T(8,128)(2,1)} %param.10, s32[1024]{0:T(1024)S(1)} %pad_clamp_fusion.1), kind=kCustom, calls=%fused_computation.1.clone | custom fusion | bytes 54529280 | tf_op jit(solution)/shard_map/jit(_take)/gather | solution.py:14
  63.0 36.9 %select_multiply_fusion.2 = (bf16[832,128,128]{2,1,0:T(8,128)(2,1)}, bf16[832,128,128]{2,1,0:T(8,128)(2,1)}) fusion(bf16[832,128,128]{2,1,0:T(8,128)(2,1)} %gather_fusion, pred[832]{0:T(1024)(128)(4,1)S(1)} %get-tuple-element.8, bf16[832]{0:T(1024)(128)(2,1)S(1)} %convert_element_type.39, bf16[832,128,128]{2,1,0:T(8,128)(2,1)} %gather_fusion.1), kind=kLoop, calls=%fused_computation.14 | loop fusion | flops 54525952 | bytes 109054400 | tf_op jit(solution)/shard_map/mul | solution.py:14
  99.9 35.0 %copy.8 = bf16[32,26,128,128]{2,0,3,1:T(8,128)(2,1)} copy(bf16[32,26,128,128]{3,2,1,0:T(8,128)(2,1)} %bitcast.51) | data formatting | bytes 54525952 | tf_op jit(solution)/shard_map/reshape | solution.py:17
  134.9 0.0 copy-start
  134.9 35.4 %copy.7 = bf16[32,26,128,128]{2,0,3,1:T(8,128)(2,1)} copy(bf16[32,26,128,128]{3,2,1,0:T(8,128)(2,1)} %bitcast.50) | data formatting | bytes 54525952 | tf_op jit(solution)/shard_map/reshape | solution.py:17
  170.3 0.0 copy-done
  170.3 0.1 reshape.75
  170.3 0.3 reduce-window.24
  170.6 0.1 slice.23
  170.7 0.0 all-gather.2.cloned.1.call-done
  170.7 24.7 %fusion.23 = bf16[512,3328]{0,1:T(8,128)(2,1)} fusion(bf16[512,4096]{1,0:T(8,128)(2,1)} %all-gather.2.cloned.1.call-done, bf16[416,8,32,128]{3,2,1,0:T(8,128)(2,1)} %bitcast.52), kind=kOutput, calls=%fused_computation.25 | convolution fusion | flops 13960347648 | bytes 34865152 | tf_op jit(solution)/shard_map/dot_general | solution.py:27
  195.5 24.5 %fusion.26 = bf16[512,3328]{0,1:T(8,128)(2,1)} fusion(bf16[512,4096]{1,0:T(8,128)(2,1)} %all-gather.2.cloned.1.call-done, bf16[416,8,32,128]{3,2,1,0:T(8,128)(2,1)} %bitcast.53), kind=kOutput, calls=%fused_computation.26 | convolution fusion | flops 13960347648 | bytes 34865152 | tf_op jit(solution)/shard_map/dot_general | solution.py:26
  219.9 0.0 all-reduce.5.cloned.1.call-update
  220.0 0.0 reduce-scatter.2.cloned.1.call-start
  220.0 0.1 slice_reduce_fusion
  220.1 0.1 add_bitcast_fusion
  220.2 28.0 %gather_fusion.2 = bf16[832,128,128]{2,1,0:T(8,128)(2,1)} fusion(bf16[640,128,128]{2,1,0:T(8,128)(2,1)} %param.11, s32[1024]{0:T(1024)S(1)} %pad_clamp_fusion), kind=kCustom, calls=%fused_computation.2.clone | custom fusion | bytes 54529280 | tf_op jit(solution)/shard_map/jit(_take)/gather | solution.py:14
  248.3 18.3 %select_multiply_fusion = bf16[832,128,128]{2,1,0:T(8,128)(2,1)} fusion(bf16[832,128,128]{2,1,0:T(8,128)(2,1)} %gather_fusion.2, pred[832]{0:T(1024)(128)(4,1)S(1)} %get-tuple-element.10, bf16[832]{0:T(1024)(128)(2,1)S(1)} %convert_element_type.47), kind=kLoop, calls=%fused_computation.12 | loop fusion | flops 27262976 | bytes 54528448 | tf_op jit(solution)/shard_map/mul | solution.py:14
  266.6 24.4 %copy.9 = bf16[26,32,128,128]{3,1,2,0:T(8,128)(2,1)} copy(bf16[26,32,128,128]{3,2,1,0:T(8,128)(2,1)} %bitcast.49) | data formatting | bytes 54525952 | tf_op jit(solution)/shard_map/reshape | solution.py:17
  291.0 61.4 %all-reduce.5.cloned.1.call-done = (bf16[512,3328]{0,1:T(8,128)(2,1)}, bf16[512,3328]{0,1:T(8,128)(2,1)}) async-done(((bf16[512,3328]{0,1:T(8,128)(2,1)}, bf16[512,3328]{0,1:T(8,128)(2,1)}), (bf16[512,3328]{0,1:T(8,128)(2,1)}, bf16[512,3328]{0,1:T(8,128)(2,1)})) %all-reduce.5.cloned.1.call-update) | async-done | bytes 6815760 | tf_op jit(solution)/shard_map/psum | solution.py:30
  352.4 26.2 %fusion.20 = bf16[512,4096]{1,0:T(8,128)(2,1)} fusion(bf16[416,8,32,128]{3,2,1,0:T(8,128)(2,1)} %bitcast.54, bf16[512,3328]{0,1:T(8,128)(2,1)} %get-tuple-element.6, bf16[512,3328]{0,1:T(8,128)(2,1)} %get-tuple-element.7), kind=kOutput, calls=%fused_computation.24 | convolution fusion | flops 13974372352 | bytes 38273024 | tf_op jit(solution)/shard_map/dot_general | solution.py:33
  378.5 0.0 reduce-scatter.2.cloned.1.call-update
  378.6 88.9 %reduce-scatter.2.cloned.1.call-done = bf16[64,4096]{1,0:T(8,128)(2,1)} async-done(((bf16[512,4096]{1,0:T(8,128)(2,1)}), bf16[64,4096]{1,0:T(8,128)(2,1)}) %reduce-scatter.2.cloned.1.call-update) | async-done | bytes 524304 | tf_op jit(solution)/shard_map/reduce_scatter | solution.py:34
  (10 shorter events, 0.1 us)
Async XLA Ops:
  6.5 164.2 %all-gather.2.cloned.1.call-start = ((), (), s32[]{:S(2)}) async-start(), calls=%async_computation.1 | async-start | bytes 4718592 | tf_op jit(solution)/shard_map/all_gather | solution.py:25
  7.3 345.1 %all-reduce.5.cloned.1.call-start = ((), (), s32[]{:S(2)}) async-start(), calls=%async_computation.3 | async-start | bytes 13631488 | tf_op jit(solution)/shard_map/psum | solution.py:30
  134.9 35.4 %copy-start = (s32[26,32]{1,0:T(8,128)S(1)}, s32[26,32]{1,0:T(8,128)}, u32[]{:S(2)}) copy-start(s32[26,32]{1,0:T(8,128)} %param.13) | copy-start | bytes 9988
  220.0 247.5 %reduce-scatter.2.cloned.1.call-start = ((), (), s32[]{:S(2)}) async-start(), calls=%async_computation.2 | async-start | bytes 4718592 | tf_op jit(solution)/shard_map/reduce_scatter | solution.py:34
Sparse Core Ops, SparseCore 0:
  9.5 76.0 all-gather.1
  220.1 132.2 all-reduce.4
  378.7 88.7 reduce-scatter.1
where the time goes:
time: 482 us; the launch traced here: 474 us
  local copies, waits for them, and re-layouts  178 us (37%)
  waiting for transfers between devices  151 us (31%)
  matrix products  75.4 us (16%)
  other arithmetic  56.1 us (12%)
  between operations  13.4 us (3%)
    reshape x3, local copies, waits for them, and re-layouts, dense_tile(): picked.reshape(in_blocks, out_blocks, block, block).transpose(0, 2, 1, 3)  94.8 us
    reduce_scatter x1, waiting for transfers between devices, local(): lax.psum_scatter(partial_out.astype(jnp.bfloat16), 'col', scatter_dimensi...  88.9 us
    gather x3, local copies, waits for them, and re-layouts, dense_tile(): jnp.take(packed_tile, slot_index, axis=0)  82.2 us
    psum x1, waiting for transfers between devices, local(): lax.psum(up_rows.astype(jnp.bfloat16), 'row').astype(jnp.float32)  61.4 us
    mul x2, other arithmetic, dense_tile(): jnp.take(packed_tile, slot_index, axis=0)  55.2 us
    dot_general x1, matrix products, local(): jnp.dot(every_hidden, down_dense, preferred_element_type=jnp.float32)  26.2 us
    dot_general x1, matrix products, local(): up_rows = jnp.dot(segment, up_dense, preferred_element_type=jnp.float32)  24.7 us
    dot_general x1, matrix products, local(): gate_rows = jnp.dot(segment, gate_dense, preferred_element_type=jnp.float32)  24.5 us
  transfers between devices with their start and end apart: 3, of which 2 were waited for; matrix products, arithmetic and copies ran while one was open for 49% of the time, Pallas kernels for 0%

commit v1 on v0

--- a/solution.py
+++ b/solution.py
@@ -2,6 +2,12 @@
 import jax.numpy as jnp
 from jax import lax
 from jax.sharding import PartitionSpec as P
+
+
+def summed_here(shard, axis):
+    terms = lax.all_gather(shard, axis, axis=0, tiled=False)
+    summed = terms.sum(axis=0)
+    return summed
 
 
 def dense_tile(packed_tile, keep_tile):
@@ -27,7 +33,7 @@
     up_rows = jnp.dot(segment, up_dense, preferred_element_type=jnp.float32)
     gate_sum, up_sum = (
         lax.psum(gate_rows.astype(jnp.bfloat16), "row").astype(jnp.float32),
-        lax.psum(up_rows.astype(jnp.bfloat16), "row").astype(jnp.float32),
+        summed_here(up_rows.astype(jnp.bfloat16), "row").astype(jnp.float32),
     )
     every_hidden = (jax.nn.silu(gate_sum) * up_sum).astype(jnp.bfloat16)
     partial_out = jnp.dot(every_hidden, down_dense, preferred_element_type=jnp.float32)

time: 482 us -> 470 us (0.975)
  waiting for transfers between devices: 151 us -> 92.9 us
  local copies, waits for them, and re-layouts: 178 us -> 203 us
  other arithmetic: 56.1 us -> 78.9 us
    psum x1, waiting for transfers between devices: 61.4 us -> 0.02 us  [local(): lax.psum(gate_rows.astype(jnp.bfloat16), 'row').astype(jnp.float32)]
    all_gather x0 -> x1, local copies, waits for them, and re-layouts: none -> 23.1 us  [summed_here(): terms = lax.all_gather(shard, axis, axis=0, tiled=False)]
    reduce_sum x0 -> x1, other arithmetic: none -> 21.4 us  [summed_here(): summed = terms.sum(axis=0)]
  transfers between devices with their start and end apart: 3 -> 4, of which waited for: 2 -> 1; matrix products, arithmetic and copies ran while one was open for 49% -> 66% of each run, Pallas kernels for 0% -> 0%
where the time goes in v1:
time: 470 us; the launch traced here: 462 us
  local copies, waits for them, and re-layouts  203 us (43%)
  waiting for transfers between devices  92.9 us (20%)
  other arithmetic  78.9 us (17%)
  matrix products  74.1 us (16%)
  between operations  13.4 us (3%)
    reshape x3, local copies, waits for them, and re-layouts, dense_tile(): picked.reshape(in_blocks, out_blocks, block, block).transpose(0, 2, 1, 3)  96.1 us
    reduce_scatter x1, waiting for transfers between devices, local(): lax.psum_scatter(partial_out.astype(jnp.bfloat16), 'col', scatter_dimensi...  92.1 us
    gather x3, local copies, waits for them, and re-layouts, dense_tile(): jnp.take(packed_tile, slot_index, axis=0)  82 us
    mul x2, other arithmetic, dense_tile(): jnp.take(packed_tile, slot_index, axis=0)  56.6 us
    dot_general x1, matrix products, local(): jnp.dot(every_hidden, down_dense, preferred_element_type=jnp.float32)  25.1 us
    dot_general x1, matrix products, local(): up_rows = jnp.dot(segment, up_dense, preferred_element_type=jnp.float32)  24.7 us
    dot_general x1, matrix products, local(): gate_rows = jnp.dot(segment, gate_dense, preferred_element_type=jnp.float32)  24.3 us
    all_gather x1, local copies, waits for them, and re-layouts, summed_here(): terms = lax.all_gather(shard, axis, axis=0, tiled=False)  23.1 us
  transfers between devices with their start and end apart: 4, of which 1 were waited for; matrix products, arithmetic and copies ran while one was open for 66% of the time, Pallas kernels for 0%

profile of v1, /device:TPU:0, one launch (start us, length us, event | category | flops | bytes accessed | tf_op | source)
XLA Modules:
  0.0 462.0 jit_solution(12038373193838142047)
XLA Ops:
  6.5 0.0 all-gather.4.cloned.1.call-start
  6.5 0.7 all-gather.4.cloned.1.call-update
  7.3 0.0 all-gather.6.cloned.1.call-start
  7.3 0.8 reshape.68
  8.1 0.3 reduce-window.16
  8.4 0.1 slice.20
  8.5 0.1 slice_reduce_fusion.1
  8.6 0.1 add_bitcast_fusion.1
  8.7 27.2 %gather_fusion = bf16[832,128,128]{2,1,0:T(8,128)(2,1)} fusion(bf16[640,128,128]{2,1,0:T(8,128)(2,1)} %param.9, s32[1024]{0:T(1024)S(1)} %pad_clamp_fusion.1), kind=kCustom, calls=%fused_computation.clone | custom fusion | bytes 54529280 | tf_op jit(solution)/shard_map/jit(_take)/gather | solution.py:20
  35.9 27.1 %gather_fusion.1 = bf16[832,128,128]{2,1,0:T(8,128)(2,1)} fusion(bf16[640,128,128]{2,1,0:T(8,128)(2,1)} %param.10, s32[1024]{0:T(1024)S(1)} %pad_clamp_fusion.1), kind=kCustom, calls=%fused_computation.1.clone | custom fusion | bytes 54529280 | tf_op jit(solution)/shard_map/jit(_take)/gather | solution.py:20
  62.9 36.9 %select_multiply_fusion.2 = (bf16[832,128,128]{2,1,0:T(8,128)(2,1)}, bf16[832,128,128]{2,1,0:T(8,128)(2,1)}) fusion(bf16[832,128,128]{2,1,0:T(8,128)(2,1)} %gather_fusion, pred[832]{0:T(1024)(128)(4,1)S(1)} %get-tuple-element.6, bf16[832]{0:T(1024)(128)(2,1)S(1)} %convert_element_type.41, bf16[832,128,128]{2,1,0:T(8,128)(2,1)} %gather_fusion.1), kind=kLoop, calls=%fused_computation.14 | loop fusion | flops 54525952 | bytes 109054400 | tf_op jit(solution)/shard_map/mul | solution.py:20
  99.9 35.4 %copy.8 = bf16[32,26,128,128]{2,0,3,1:T(8,128)(2,1)} copy(bf16[32,26,128,128]{3,2,1,0:T(8,128)(2,1)} %bitcast.53) | data formatting | bytes 54525952 | tf_op jit(solution)/shard_map/reshape | solution.py:23
  135.2 0.0 all-gather.4.cloned.1.call-done
  135.2 24.7 %fusion.23 = bf16[512,3328]{0,1:T(8,128)(2,1)} fusion(bf16[512,4096]{1,0:T(8,128)(2,1)} %all-gather.4.cloned.1.call-done, bf16[416,8,32,128]{3,2,1,0:T(8,128)(2,1)} %bitcast.56), kind=kOutput, calls=%fused_computation.25 | convolution fusion | flops 13960347648 | bytes 34865152 | tf_op jit(solution)/shard_map/dot_general | solution.py:33
  160.0 0.0 all-gather.6.cloned.1.call-update
  160.0 0.0 all-reduce.4.cloned.1.call-start
  160.0 0.0 copy-start
  160.1 36.3 %copy.7 = bf16[32,26,128,128]{2,0,3,1:T(8,128)(2,1)} copy(bf16[32,26,128,128]{3,2,1,0:T(8,128)(2,1)} %bitcast.52) | data formatting | bytes 54525952 | tf_op jit(solution)/shard_map/reshape | solution.py:23
  196.4 0.0 copy-done
  196.4 0.1 reshape.75
  196.5 0.3 reduce-window.24
  196.7 0.1 slice.23
  196.8 0.1 slice_reduce_fusion
  197.0 0.1 add_bitcast_fusion
  197.1 27.8 %gather_fusion.2 = bf16[832,128,128]{2,1,0:T(8,128)(2,1)} fusion(bf16[640,128,128]{2,1,0:T(8,128)(2,1)} %param.11, s32[1024]{0:T(1024)S(1)} %pad_clamp_fusion), kind=kCustom, calls=%fused_computation.2.clone | custom fusion | bytes 54529280 | tf_op jit(solution)/shard_map/jit(_take)/gather | solution.py:20
  224.9 24.3 %fusion.26 = bf16[512,3328]{0,1:T(8,128)(2,1)} fusion(bf16[512,4096]{1,0:T(8,128)(2,1)} %all-gather.4.cloned.1.call-done, bf16[416,8,32,128]{3,2,1,0:T(8,128)(2,1)} %bitcast.54), kind=kOutput, calls=%fused_computation.26 | convolution fusion | flops 13960347648 | bytes 34865152 | tf_op jit(solution)/shard_map/dot_general | solution.py:32
  249.1 0.0 all-reduce.4.cloned.1.call-update
  249.2 0.0 reduce-scatter.2.cloned.1.call-start
  249.2 19.7 %select_multiply_fusion = bf16[832,128,128]{2,1,0:T(8,128)(2,1)} fusion(bf16[832,128,128]{2,1,0:T(8,128)(2,1)} %gather_fusion.2, pred[832]{0:T(1024)(128)(4,1)S(1)} %get-tuple-element.8, bf16[832]{0:T(1024)(128)(2,1)S(1)} %convert_element_type.49), kind=kLoop, calls=%fused_computation.12 | loop fusion | flops 27262976 | bytes 54528448 | tf_op jit(solution)/shard_map/mul | solution.py:20
  268.9 24.4 %copy.9 = bf16[26,32,128,128]{3,1,2,0:T(8,128)(2,1)} copy(bf16[26,32,128,128]{3,2,1,0:T(8,128)(2,1)} %bitcast.51) | data formatting | bytes 54525952 | tf_op jit(solution)/shard_map/reshape | solution.py:23
  293.4 0.0 all-gather.6.cloned.1.call-done
  293.4 23.1 %reshape.104 = bf16[4,512,3328]{1,0,2:T(4,128)(2,1)} reshape(bf16[2048,3328]{0,1:T(8,128)(2,1)} %all-gather.6.cloned.1.call-done) | data formatting | bytes 27262976 | tf_op jit(solution)/shard_map/all_gather | solution.py:8
  316.5 21.4 %reduce_sum.12 = bf16[512,3328]{0,1:T(8,128)(2,1)S(1)} reduce(bf16[4,512,3328]{1,0,2:T(4,128)(2,1)} %reshape.104, bf16[]{:T(256)} %constant.27.clone.1), dimensions={0}, to_apply=%region_3.5 | reduce | flops 5111808 | bytes 17039362 | tf_op jit(solution)/shard_map/reduce_sum | solution.py:9
  337.9 0.0 all-reduce.4.cloned.1.call-done
  337.9 25.1 %fusion.20 = bf16[512,4096]{1,0:T(8,128)(2,1)} fusion(bf16[416,8,32,128]{3,2,1,0:T(8,128)(2,1)} %bitcast.55, bf16[512,3328]{0,1:T(8,128)(2,1)S(1)} %reduce_sum.12, bf16[512,3328]{0,1:T(8,128)(2,1)} %all-reduce.4.cloned.1.call-done), kind=kOutput, calls=%fused_computation.24 | convolution fusion | flops 13974372352 | bytes 38273024 | tf_op jit(solution)/shard_map/dot_general | solution.py:39
  363.1 0.0 reduce-scatter.2.cloned.1.call-update
  363.1 92.1 %reduce-scatter.2.cloned.1.call-done = bf16[64,4096]{1,0:T(8,128)(2,1)} async-done(((bf16[512,4096]{1,0:T(8,128)(2,1)}), bf16[64,4096]{1,0:T(8,128)(2,1)}) %reduce-scatter.2.cloned.1.call-update) | async-done | bytes 524304 | tf_op jit(solution)/shard_map/reduce_scatter | solution.py:40
  (10 shorter events, 0.1 us)
Async XLA Ops:
  6.5 128.7 %all-gather.4.cloned.1.call-start = ((), (), s32[]{:S(2)}) async-start(), calls=%async_computation.1 | async-start | bytes 4718592 | tf_op jit(solution)/shard_map/all_gather | solution.py:31
  7.3 286.1 %all-gather.6.cloned.1.call-start = ((), (), s32[]{:S(2)}) async-start(), calls=%async_computation.4 | async-start | bytes 17039360 | tf_op jit(solution)/shard_map/all_gather | solution.py:8
  160.0 177.9 %all-reduce.4.cloned.1.call-start = ((), (), s32[]{:S(2)}) async-start(), calls=%async_computation.2 | async-start | bytes 6815744 | tf_op jit(solution)/shard_map/psum | solution.py:35
  160.0 36.3 %copy-start = (s32[26,32]{1,0:T(8,128)S(1)}, s32[26,32]{1,0:T(8,128)}, u32[]{:S(2)}) copy-start(s32[26,32]{1,0:T(8,128)} %param.13) | copy-start | bytes 9988
  249.2 206.1 %reduce-scatter.2.cloned.1.call-start = ((), (), s32[]{:S(2)}) async-start(), calls=%async_computation.3 | async-start | bytes 4718592 | tf_op jit(solution)/shard_map/reduce_scatter | solution.py:40
Sparse Core Ops, SparseCore 0:
  9.5 76.0 all-gather.3
  160.1 91.6 all-gather.5
  254.2 72.6 all-reduce.3
  363.2 91.9 reduce-scatter.1
